TPU v7x, 256 devices: a whole 4x4x8 slice. The times are simulated.
256 devices in a mesh: dp: 16 (over z, core), expert: 16 (over x, y).
Axes of the slice: x: 4, y: 4, z: 8, core: 2. Of those that a mesh axis runs over, the one named last changes fastest.
Arguments:
- tokens: bfloat16 [32768, 2048], P(('dp', 'expert')), may hold values from -24 to 24
- cotangent: bfloat16 [32768, 2048], P(('dp', 'expert')), may hold values from -6 to 6
- expert_ids: int32 [32768, 2], P(('dp', 'expert')), may hold values from 0 to 15, all different within a row; in each aligned block of 128 rows (0 to 127, 128 to 255, ...) at most 24 rows name the same one
- placed: int32 [16], replicated, may hold values from 0 to 15, as said below
- router_weight: bfloat16 [2048, 16], replicated, may hold values from -0.125 to 0.125
- gate_weight: bfloat16 [16, 2048, 768], P('expert', 'dp'), may hold values from -0.125 to 0.125
- up_weight: bfloat16 [16, 2048, 768], P('expert', 'dp'), may hold values from -0.125 to 0.125
- down_weight: bfloat16 [16, 2048, 768], P('expert', 'dp'), may hold values from -0.21875 to 0.21875
Outputs:
- mixed: bfloat16 [32768, 2048], P(('dp', 'expert'))
- token_grad: bfloat16 [32768, 2048], P(('dp', 'expert'))
- gate_grad: bfloat16 [16, 2048, 768], P('expert', 'dp')
- up_grad: bfloat16 [16, 2048, 768], P('expert', 'dp')
- down_grad: bfloat16 [16, 2048, 768], P('expert', 'dp')
- router_grad: float32 [2048, 16], replicated
Inputs may be any that keep to these rules, and one draw needn't show every extreme that they name: `expert_ids`: within the rows of one device (128 tokens, two experts each) no expert is named by more than 24 rows, and in some device some expert is named by exactly 24; a token names two different experts. placed is its own inverse, and placed[d] equals d or differs from d in exactly one bit.
All inputs are finite; a program needn't handle non-finite values.
Results may differ from a plain program's by a relative error of at most 0.018.
Values may be sent and summed in bfloat16 or wider, within the bound.
No kernel may reach another device: no remote copies, remote signals or barrier semaphores. Data moves between devices by JAX's collectives and lax.ppermute only.
A program may use at most 128 MiB of HBM per device.

v0:
```python
import jax
import jax.numpy as jnp
from jax import lax
from jax.sharding import PartitionSpec as P
from jax.experimental.layout import Layout, with_layout_constraint


def swapped(array, axis, stride):
    return lax.ppermute(array, axis, [(i, i ^ 1 << stride) for i in range(lax.axis_size(axis))])


def gather_by_exchange(piece, axis):
    count = lax.axis_size(axis)
    copies = jnp.broadcast_to(piece[None], (count,) + piece.shape)
    joined = lax.all_to_all(copies, axis, 0, 0, tiled=True)
    return joined.reshape((count * piece.shape[0],) + piece.shape[1:])


def reduce_router(term, companion, partner, my_index):
    groups = lax.axis_size("expert")
    replicas = lax.axis_size("dp")
    rows = term.shape[0]
    parts = lax.all_to_all(
        term.reshape(groups, rows // groups, term.shape[1]), "expert", 0, 0, tiled=True
    )
    piece = jnp.sum(parts, axis=0)
    piece, companion = lax.optimization_barrier((piece, companion))
    arrivals = [
        swapped(companion, "expert", bit_level) for bit_level in range(groups.bit_length() - 1)
    ]
    for bit_level in range(replicas.bit_length() - 1):
        piece = piece + swapped(piece, "dp", bit_level)
    piece, arrivals = lax.optimization_barrier((piece, arrivals))
    chosen = companion
    for bit_level, arrived in enumerate(arrivals):
        chosen = jnp.where(partner == jnp.bitwise_xor(my_index, 1 << bit_level), arrived, chosen)
    return (gather_by_exchange(piece, "expert"), chosen)


def gate_values(logits, picked):
    scores = jax.nn.sigmoid(logits)
    chosen = jnp.sum(scores[:, None, :] * picked, axis=2)
    return chosen / jnp.sum(chosen, axis=1, keepdims=True)


def slot_numbers(expert_ids, holder, capacity, devices):
    labels = jnp.arange(devices, dtype=jnp.int32)
    member_e = (expert_ids[:, :, None] == labels[None, None, :]).astype(jnp.int32)
    target = jnp.sum(member_e * holder[None, None, :], axis=2)
    flat_target = target.reshape(-1)
    member = (flat_target[:, None] == labels[None, :]).astype(jnp.int32)
    ranking = jnp.sum((jnp.cumsum(member, axis=0) - 1) * member, axis=1)
    return (flat_target * capacity + ranking).reshape(expert_ids.shape)


def scatter_rows(per_pair, slot_index, total):
    flat_rows = per_pair.reshape(-1, per_pair.shape[2])
    empty = jnp.zeros((total, per_pair.shape[2]), per_pair.dtype)
    return empty.at[slot_index.reshape(-1)].set(flat_rows)


def expert_forward(slot_rows, gate_full, up_full, down_full):
    pre_gate = jnp.dot(slot_rows, gate_full, preferred_element_type=jnp.float32)
    pre_up = jnp.dot(slot_rows, up_full, preferred_element_type=jnp.float32)
    hidden = (jax.nn.silu(pre_gate) * pre_up).astype(jnp.bfloat16)
    result = lax.dot_general(
        hidden, down_full, (((1,), (1,)), ((), ())), preferred_element_type=jnp.float32
    )
    return (result.astype(jnp.bfloat16), pre_gate, pre_up, hidden)


def expert_backward(d_out, pre_gate, pre_up, gate_full, up_full, down_full):
    d_hidden = jnp.dot(d_out, down_full, preferred_element_type=jnp.float32)
    sigma = jax.nn.sigmoid(pre_gate)
    d_pre_gate = (d_hidden * pre_up * sigma * (1.0 + pre_gate * (1.0 - sigma))).astype(jnp.bfloat16)
    d_pre_up = (d_hidden * pre_gate * sigma).astype(jnp.bfloat16)
    back_dims = (((1,), (1,)), ((), ()))
    d_rows = lax.dot_general(d_pre_gate, gate_full, back_dims, preferred_element_type=jnp.float32)
    d_rows = d_rows + lax.dot_general(
        d_pre_up, up_full, back_dims, preferred_element_type=jnp.float32
    )
    return (d_rows.astype(jnp.bfloat16), d_pre_gate, d_pre_up)


def row_major(array):
    return with_layout_constraint(array, Layout(major_to_minor=tuple(range(array.ndim))))


def contract_rows(left, right):
    return lax.dot_general(
        left, right, (((0,), (0,)), ((), ())), preferred_element_type=jnp.float32
    )


def on_device(
    tokens, cotangent, expert_ids, placed, router_weight, gate_weight, up_weight, down_weight
):
    count = tokens.shape[0]
    width = tokens.shape[1]
    hid_width = gate_weight.shape[2]
    groups = lax.axis_size("expert")
    replicas = lax.axis_size("dp")
    capacity = 3 * count // groups
    total = groups * capacity
    levels = groups.bit_length() - 1
    my_index = lax.axis_index("expert")
    labels = jnp.arange(groups, dtype=jnp.int32)
    partner = jnp.sum(jnp.where(labels == my_index, placed, 0))
    grad_scale = (2.0 * count * replicas) ** (-0.5)
    router_scale = (1.0 * count * replicas * groups) ** (-0.5)
    logits = jnp.dot(tokens, router_weight, preferred_element_type=jnp.float32)
    picked = (expert_ids[:, :, None] == labels[None, None, :]).astype(jnp.float32)

    def gate_of(values):
        return gate_values(values, picked)

    gate_vals, gate_vjp = jax.vjp(gate_of, logits)
    held = jnp.concatenate([gate_weight, up_weight, down_weight], axis=0)
    gathered = lax.all_gather(held, "dp", axis=1, tiled=True)
    gate_full, up_full, down_full = (gathered[0], gathered[1], gathered[2])
    slot_index = slot_numbers(expert_ids, labels, capacity, groups)
    spread = jnp.broadcast_to(tokens[:, None, :], (count, 2, width))
    outbox = scatter_rows(spread, slot_index, total).reshape(groups, capacity, width)
    received = lax.all_to_all(outbox, "expert", split_axis=0, concat_axis=0, tiled=True)
    item_count = received.shape[1]
    forward_slot_rows = received.reshape(-1, width)
    result, pre_gate, pre_up, hidden = expert_forward(
        forward_slot_rows, gate_full, up_full, down_full
    )
    result, pre_gate, pre_up, hidden, inbox = (
        result.reshape(groups, item_count, width),
        pre_gate.reshape(groups, item_count, hid_width),
        pre_up.reshape(groups, item_count, hid_width),
        hidden.reshape(groups, item_count, hid_width),
        received,
    )
    returned = lax.all_to_all(result, "expert", split_axis=0, concat_axis=0, tiled=True).reshape(
        total, width
    )
    expert_out = returned[slot_index].astype(jnp.float32)
    mixed = jnp.sum(gate_vals[:, :, None] * expert_out, axis=1).astype(jnp.bfloat16)
    cot_wide = cotangent.astype(jnp.float32)
    d_gates = jnp.sum(cot_wide[:, None, :] * expert_out, axis=2)
    d_out = (gate_vals[:, :, None] * cot_wide[:, None, :]).astype(jnp.bfloat16)
    d_outbox = scatter_rows(d_out, slot_index, total).reshape(groups, capacity, width)
    d_inbox = lax.all_to_all(d_outbox, "expert", split_axis=0, concat_axis=0, tiled=True).reshape(
        total, width
    )
    gate_back, up_back, down_back = (gate_full, up_full, down_full)
    slot_rows = inbox.reshape(total, width)
    hidden_rows = hidden.reshape(total, hid_width)
    d_rows, d_pre_gate, d_pre_up = expert_backward(
        d_inbox,
        pre_gate.reshape(total, hid_width),
        pre_up.reshape(total, hid_width),
        gate_back,
        up_back,
        down_back,
    )
    d_returned = lax.all_to_all(
        d_rows.reshape(groups, capacity, width), "expert", split_axis=0, concat_axis=0, tiled=True
    ).reshape(total, width)
    d_expert = jnp.sum(d_returned[slot_index].astype(jnp.float32), axis=1)
    pieces = [
        row_major(contract_rows(slot_rows, jnp.concatenate([d_pre_gate, d_pre_up], axis=1))),
        row_major(contract_rows(d_inbox, hidden_rows)),
    ]
    shares = lax.psum_scatter(
        (jnp.concatenate(pieces, axis=1) * grad_scale).astype(jnp.bfloat16),
        "dp",
        scatter_dimension=0,
        tiled=True,
    ).astype(jnp.float32)
    grad_stack = jnp.stack(
        [shares[:, :hid_width], shares[:, hid_width : 2 * hid_width], shares[:, 2 * hid_width :]],
        axis=0,
    ).astype(jnp.bfloat16)
    d_logits = gate_vjp(d_gates)[0].astype(jnp.bfloat16)
    router_term = contract_rows(tokens, d_logits) * router_scale
    router_grad, grad_stack = reduce_router(router_term, grad_stack, partner, my_index)
    router_back = lax.dot_general(
        d_logits, router_weight, (((1,), (1,)), ((), ())), preferred_element_type=jnp.float32
    )
    token_grad = (d_expert + router_back).astype(jnp.bfloat16)
    return (mixed, token_grad, grad_stack[0:1], grad_stack[1:2], grad_stack[2:3], router_grad)


def solution(mesh):
    in_specs = (
        P(("dp", "expert"), None),
        P(("dp", "expert"), None),
        P(("dp", "expert"), None),
        P(),
        P(),
        P("expert", "dp", None),
        P("expert", "dp", None),
        P("expert", "dp", None),
    )
    out_specs = (
        P(("dp", "expert"), None),
        P(("dp", "expert"), None),
        P("expert", "dp", None),
        P("expert", "dp", None),
        P("expert", "dp", None),
        P(),
    )
    return jax.shard_map(
        on_device, mesh=mesh, in_specs=in_specs, out_specs=out_specs, check_vma=False
    )
```

profile of v0, /device:TPU:1, one launch (start us, length us, event | category | flops | bytes accessed | tf_op | source)
XLA Modules:
  0.0 226.3 jit_solution(6985422025171004675)
XLA Ops:
  7.2 2.1 pad_maximum_fusion
  12.1 3.4 %scatter_custom_fusion = bf16[384,2048]{1,0:T(8,128)(2,1)} fusion(s32[256]{0:T(256)S(1)} %bitcast.88, bf16[256,2048]{1,0:T(8,128)(2,1)S(1)} %reshape.199, bf16[]{:T(256)} %constant.16.clone.1), kind=kCustom, calls=%fused_computation.37 | custom fusion | bytes 1572866 | tf_op jit(solution)/shard_map/scatter | solution.py:59
  15.5 7.7 %all-to-all-start = ((bf16[16,24,2048]{2,1,0:T(8,128)(2,1)}), bf16[16,24,2048]{2,1,0:T(8,128)(2,1)S(1)}, u32[]{:S(2)}, u32[]{:S(2)}) async-start(bf16[16,24,2048]{2,1,0:T(8,128)(2,1)} %bitcast.3), calls=%async_computation | async-start | bytes 3145728 | tf_op jit(solution)/shard_map/all_to_all | solution.py:124
  23.2 2.5 %mul.155 = f32[128,2,2048]{2,1,0:T(2,128)} broadcast(bf16[128,2048]{1,0:T(8,128)(2,1)S(1)} %copy-done.3), dimensions={0,2} | broadcast | bytes 2621440 | tf_op jit(solution)/shard_map/mul | solution.py:144
  25.7 3.7 %mul.156 = f32[256,2048]{1,0:T(8,128)} reshape(f32[128,2,2048]{2,1,0:T(2,128)} %mul.155) | data formatting | bytes 4194304 | tf_op jit(solution)/shard_map/mul | solution.py:144
  29.9 4.7 %scatter_custom_fusion.1 = bf16[384,2048]{1,0:T(8,128)(2,1)} fusion(s32[256]{0:T(256)S(1)} %bitcast.89, f32[256,2048]{1,0:T(8,128)} %mul.156, f32[256]{0:T(256)S(1)} %div.42, bf16[]{:T(256)} %constant.16.clone.1), kind=kCustom, calls=%fused_computation.34 | custom fusion | flops 1048576 | bytes 3671042 | tf_op jit(solution)/shard_map/scatter | solution.py:59
  34.6 9.4 %all-to-all-done = bf16[16,24,2048]{2,1,0:T(8,128)(2,1)S(1)} async-done(((bf16[16,24,2048]{2,1,0:T(8,128)(2,1)}), bf16[16,24,2048]{2,1,0:T(8,128)(2,1)S(1)}, u32[]{:S(2)}, u32[]{:S(2)}) %all-to-all-start) | async-done | bytes 1572896 | tf_op jit(solution)/shard_map/all_to_all | solution.py:124
  44.0 5.3 %all-to-all-start.2 = ((bf16[16,24,2048]{2,1,0:T(8,128)(2,1)}), bf16[16,24,2048]{2,1,0:T(8,128)(2,1)S(1)}, u32[]{:S(2)}, u32[]{:S(2)}) async-start(bf16[16,24,2048]{2,1,0:T(8,128)(2,1)} %bitcast.84), calls=%async_computation.2 | async-start | bytes 3145728 | tf_op jit(solution)/shard_map/all_to_all | solution.py:146
  49.5 25.4 %all-gather.2.cloned.1.call-done = bf16[3,2048,768]{2,1,0:T(8,128)(2,1)} async-done(((bf16[3,128,768]{2,1,0:T(8,128)(2,1)}), bf16[3,2048,768]{2,1,0:T(8,128)(2,1)}) %all-gather.2.cloned.1.call-update) | async-done | bytes 9437200 | tf_op jit(solution)/shard_map/all_gather | solution.py:119
  74.9 4.3 %fusion.2 = f32[384,768]{1,0:T(8,128)} fusion(bf16[384,2048]{1,0:T(8,128)(2,1)S(1)} %bitcast.79, bf16[3,2048,768]{2,1,0:T(8,128)(2,1)} %all-gather.2.cloned.1.call-done), kind=kOutput, calls=%fused_computation.12 | convolution fusion | flops 1207959552 | bytes 5898240 | tf_op jit(solution)/shard_map/dot_general | solution.py:63
  79.1 4.3 %fusion.3 = f32[384,768]{1,0:T(8,128)} fusion(bf16[384,2048]{1,0:T(8,128)(2,1)S(1)} %bitcast.80, bf16[3,2048,768]{2,1,0:T(8,128)(2,1)} %all-gather.2.cloned.1.call-done), kind=kOutput, calls=%fused_computation.13 | convolution fusion | flops 1207959552 | bytes 5898240 | tf_op jit(solution)/shard_map/dot_general | solution.py:64
  83.4 4.2 %multiply_convert_fusion.1 = (bf16[384,768]{1,0:T(8,128)(2,1)S(1)}, bf16[384,768]{1,0:T(8,128)(2,1)S(1)}, bf16[384,768]{1,0:T(8,128)(2,1)S(1)}) fusion(f32[384,768]{1,0:T(8,128)} %fusion.2, f32[384,768]{1,0:T(8,128)} %fusion.3, bf16[384,2048]{1,0:T(8,128)(2,1)S(1)} %bitcast.82, bf16[3,2048,768]{2,1,0:T(8,128)(2,1)} %all-gather.2.cloned.1.call-done), kind=kOutput, calls=%fused_computation.25 | convolution fusion | flops 1212678144 | bytes 8847360 | tf_op jit(solution)/shard_map/dot_general | solution.py:73
  87.7 1.8 fusion.27
  89.6 3.5 %fusion.6 = f32[2048,1536]{1,0:T(8,128)S(1)} fusion(bf16[384,2048]{1,0:T(8,128)(2,1)S(1)} %bitcast.81, bf16[384,768]{1,0:T(8,128)(2,1)S(1)} %get-tuple-element.24, bf16[384,768]{1,0:T(8,128)(2,1)S(1)} %get-tuple-element.25), kind=kOutput, calls=%fused_computation.21 | convolution fusion | flops 2418278400 | bytes 15335424 | tf_op jit(solution)/shard_map/dot_general | solution.py:90
  93.1 4.8 %fusion = bf16[2048,2304]{1,0:T(8,128)(2,1)} fusion(f32[2048,768]{1,0:T(8,128)S(1)} %fusion.27, f32[2048,1536]{1,0:T(8,128)S(1)} %fusion.6), kind=kLoop, calls=%fused_computation.5 | loop fusion | flops 14155776 | bytes 28311552 | tf_op jit(solution)/shard_map/convert_element_type | solution.py:169
  98.0 1.0 copy-done.10
  99.0 4.5 %convolution_convert_fusion = bf16[384,2048]{1,0:T(8,128)(2,1)} fusion(bf16[384,768]{1,0:T(8,128)(2,1)S(1)} %copy-done.10, bf16[3,2048,768]{2,1,0:T(8,128)(2,1)} %all-gather.2.cloned.1.call-done), kind=kOutput, calls=%fused_computation.10 | convolution fusion | flops 1208745984 | bytes 5308416 | tf_op jit(solution)/shard_map/dot_general | solution.py:66
  103.5 6.7 %all-to-all-start.1 = ((bf16[16,24,2048]{2,1,0:T(8,128)(2,1)}), bf16[16,24,2048]{2,1,0:T(8,128)(2,1)S(1)}, u32[]{:S(2)}, u32[]{:S(2)}) async-start(bf16[16,24,2048]{2,1,0:T(8,128)(2,1)} %bitcast.86), calls=%async_computation.1 | async-start | bytes 3145728 | tf_op jit(solution)/shard_map/all_to_all | solution.py:137
  110.4 1.1 convert_element_type.54
  111.8 5.0 %fusion.1 = f32[384,2048]{1,0:T(8,128)} fusion(bf16[384,768]{1,0:T(8,128)(2,1)S(1)} %copy-done.8, bf16[3,2048,768]{2,1,0:T(8,128)(2,1)} %all-gather.2.cloned.1.call-done), kind=kOutput, calls=%fused_computation.11 | convolution fusion | flops 1207959552 | bytes 6881280 | tf_op jit(solution)/shard_map/dot_general | solution.py:78
  116.8 16.2 %all-to-all-done.1 = bf16[16,24,2048]{2,1,0:T(8,128)(2,1)S(1)} async-done(((bf16[16,24,2048]{2,1,0:T(8,128)(2,1)}), bf16[16,24,2048]{2,1,0:T(8,128)(2,1)S(1)}, u32[]{:S(2)}, u32[]{:S(2)}) %all-to-all-start.1) | async-done | bytes 1572896 | tf_op jit(solution)/shard_map/all_to_all | solution.py:137
  133.0 2.4 %gather_fusion = bf16[256,2048]{1,0:T(8,128)(2,1)} fusion(bf16[384,2048]{1,0:T(8,128)(2,1)S(1)} %bitcast.78, s32[1024]{0:T(1024)S(1)} %pad_clamp_fusion), kind=kCustom, calls=%fused_computation | custom fusion | bytes 2098176 | tf_op jit(solution)/shard_map/gather | solution.py:140
  135.4 2.4 %reshape.213 = f32[128,2,2048]{2,1,0:T(2,128)S(1)} reshape(bf16[256,2048]{1,0:T(8,128)(2,1)} %gather_fusion) | data formatting | bytes 3145728 | tf_op jit(solution)/shard_map/convert_element_type | solution.py:140
  137.8 6.0 %multiply_reduce_fusion = (f32[128,2]{1,0:T(8,128)S(1)}, bf16[128,2048]{1,0:T(8,128)(2,1)}) fusion(f32[128,2,2048]{2,1,0:T(2,128)S(1)} %reshape.213, f32[128,2048]{1,0:T(8,128)} %convert_element_type.54, f32[128,2]{1,0:T(8,128)S(1)} %copy.38), kind=kLoop, calls=%fused_computation.18 | loop fusion | flops 1834752 | bytes 3672064 | tf_op jit(solution)/shard_map/reduce_sum | solution.py:143
  144.9 3.6 %all-to-all-start.4 = ((f32[16,128,16]{1,2,0:T(8,128)}), f32[16,128,16]{1,2,0:T(8,128)S(1)}, u32[]{:S(2)}, u32[]{:S(2)}) async-start(f32[16,128,16]{1,2,0:T(8,128)} %bitcast.76), calls=%async_computation.4 | async-start | bytes 262144 | tf_op jit(solution)/shard_map/all_to_all | solution.py:23
  148.4 5.6 %add_convert_fusion = bf16[384,2048]{1,0:T(8,128)(2,1)} fusion(f32[384,2048]{1,0:T(8,128)} %fusion.1, bf16[384,768]{1,0:T(8,128)(2,1)S(1)} %copy-done.6, bf16[3,2048,768]{2,1,0:T(8,128)(2,1)} %all-gather.2.cloned.1.call-done), kind=kOutput, calls=%fused_computation.9 | convolution fusion | flops 1209532416 | bytes 8454144 | tf_op jit(solution)/shard_map/dot_general | solution.py:79
  154.1 1.1 all-to-all-done.4
  155.2 5.5 %all-to-all-start.3 = ((bf16[16,24,2048]{2,1,0:T(8,128)(2,1)}), bf16[16,24,2048]{2,1,0:T(8,128)(2,1)S(1)}, u32[]{:S(2)}, u32[]{:S(2)}) async-start(bf16[16,24,2048]{2,1,0:T(8,128)(2,1)} %bitcast.85), calls=%async_computation.3 | async-start | bytes 3145728 | tf_op jit(solution)/shard_map/all_to_all | solution.py:160
  160.8 6.2 %reduce-scatter.2.cloned.1.call-done = bf16[128,2304]{1,0:T(8,128)(2,1)} async-done(((bf16[2048,2304]{1,0:T(8,128)(2,1)}), bf16[128,2304]{1,0:T(8,128)(2,1)}) %reduce-scatter.2.cloned.1.call-update) | async-done | bytes 589840 | tf_op jit(solution)/shard_map/reduce_scatter | solution.py:168
  167.0 1.2 slice_bitcast_fusion.11
  168.1 0.9 pad_maximum_fusion.1
  169.0 1.3 collective-permute-start.4
  170.3 2.2 collective-permute-start.5
  172.5 1.1 collective-permute-start.6
  173.7 2.5 %collective-permute-start.7 = (bf16[3,128,768]{2,1,0:T(8,128)(2,1)}, bf16[3,128,768]{2,1,0:T(8,128)(2,1)}, u32[]{:S(2)}, u32[]{:S(2)}) collective-permute-start(bf16[3,128,768]{2,1,0:T(8,128)(2,1)} %pad_maximum_fusion.1), channel_id=1, source_target_pairs={{0,8},{1,9},{2,10},{3,11},{4,12},{5,13},{6,14},{7,15},{8,0},{9,1},... | collective-permute-start | bytes 1769480 | tf_op jit(solution)/shard_map/ppermute | solution.py:9
  176.2 4.3 %collective-permute-start = (f32[128,16]{0,1:T(8,128)S(1)}, f32[128,16]{0,1:T(8,128)S(1)}, u32[]{:S(2)}, u32[]{:S(2)}) collective-permute-start(f32[128,16]{0,1:T(8,128)S(1)} %reduce_sum.123), channel_id=1, source_target_pairs={{0,16},{16,0},{32,48},{48,32},{64,80},{80,64},{96,112},{112,96},{1... | collective-permute-start | bytes 24584 | tf_op jit(solution)/shard_map/ppermute | solution.py:9
  181.3 2.9 %collective-permute-done.1 = f32[128,16]{0,1:T(8,128)S(1)} collective-permute-done((f32[128,16]{0,1:T(8,128)S(1)}, f32[128,16]{0,1:T(8,128)S(1)}, u32[]{:S(2)}, u32[]{:S(2)}) %collective-permute-start.1) | collective-permute-done | bytes 8224 | tf_op jit(solution)/shard_map/ppermute | solution.py:9
  184.2 1.2 collective-permute-start.2
  188.6 2.3 %gather_fusion.1 = bf16[256,2048]{1,0:T(8,128)(2,1)} fusion(bf16[384,2048]{1,0:T(8,128)(2,1)S(1)} %bitcast.77, s32[1024]{0:T(1024)S(1)} %pad_clamp_fusion), kind=kCustom, calls=%fused_computation.1 | custom fusion | bytes 2098176 | tf_op jit(solution)/shard_map/gather | solution.py:163
  191.0 2.4 %reshape.214 = f32[128,2,2048]{2,1,0:T(2,128)S(1)} reshape(bf16[256,2048]{1,0:T(8,128)(2,1)} %gather_fusion.1) | data formatting | bytes 3145728 | tf_op jit(solution)/shard_map/convert_element_type | solution.py:163
  193.4 2.8 %reduce_sum.118 = f32[128,2048]{1,0:T(8,128)S(1)} reduce(f32[128,2,2048]{2,1,0:T(2,128)S(1)} %reshape.214, f32[]{:T(128)} %constant.15.clone.1), dimensions={1}, to_apply=%region_9.10 | reduce | flops 262144 | bytes 3145732 | tf_op jit(solution)/shard_map/reduce_sum | solution.py:163
  196.2 2.5 %collective-permute-start.3 = (f32[128,16]{0,1:T(8,128)S(1)}, f32[128,16]{0,1:T(8,128)S(1)}, u32[]{:S(2)}, u32[]{:S(2)}) collective-permute-start(f32[128,16]{0,1:T(8,128)S(1)} %add.87), channel_id=1, source_target_pairs={{0,128},{16,144},{32,160},{48,176},{64,192},{80,208},{96,224},{112... | collective-permute-start | bytes 24584 | tf_op jit(solution)/shard_map/ppermute | solution.py:9
  198.7 1.1 fusion.5
  199.8 2.9 %collective-permute-done.3 = f32[128,16]{0,1:T(8,128)S(1)} collective-permute-done((f32[128,16]{0,1:T(8,128)S(1)}, f32[128,16]{0,1:T(8,128)S(1)}, u32[]{:S(2)}, u32[]{:S(2)}) %collective-permute-start.3) | collective-permute-done | bytes 8224 | tf_op jit(solution)/shard_map/ppermute | solution.py:9
  202.7 4.4 %collective-permute-done.5 = bf16[3,128,768]{2,1,0:T(8,128)(2,1)} collective-permute-done((bf16[3,128,768]{2,1,0:T(8,128)(2,1)}, bf16[3,128,768]{2,1,0:T(8,128)(2,1)}, u32[]{:S(2)}, u32[]{:S(2)}) %collective-permute-start.5) | collective-permute-done | bytes 589856 | tf_op jit(solution)/shard_map/ppermute | solution.py:9
  207.7 4.4 %all-to-all-start.5 = ((f32[16,128,16]{1,2,0:T(8,128)}), f32[16,128,16]{1,2,0:T(8,128)S(1)}, u32[]{:S(2)}, u32[]{:S(2)}) async-start(f32[16,128,16]{1,2,0:T(8,128)} %broadcast_in_dim.19), calls=%async_computation.6 | async-start | bytes 262144 | tf_op jit(solution)/shard_map/all_to_all | solution.py:15
  212.1 1.2 select_select_fusion
  214.1 4.6 %all-to-all-done.5 = f32[16,128,16]{1,2,0:T(8,128)S(1)} async-done(((f32[16,128,16]{1,2,0:T(8,128)}), f32[16,128,16]{1,2,0:T(8,128)S(1)}, u32[]{:S(2)}, u32[]{:S(2)}) %all-to-all-start.5) | async-done | bytes 131104 | tf_op jit(solution)/shard_map/all_to_all | solution.py:15
  (82 shorter events, 8.7 us)
Async XLA Ops:
  7.2 22.2 %copy-start = (bf16[2048,16]{0,1:T(8,128)(2,1)S(1)}, bf16[2048,16]{0,1:T(8,128)(2,1)}, u32[]{:S(2)}) copy-start(bf16[2048,16]{0,1:T(8,128)(2,1)} %param.12) | copy-start | bytes 196612
  7.2 2.2 copy-start.11
  7.2 3.7 %copy-start.1 = (bf16[128,2048]{1,0:T(8,128)(2,1)S(1)}, bf16[128,2048]{1,0:T(8,128)(2,1)}, u32[]{:S(2)}) copy-start(bf16[128,2048]{1,0:T(8,128)(2,1)} %param.8) | copy-start | bytes 1572868
  7.2 67.7 %all-gather.2.cloned.1.call-start = ((), (), s32[]{:S(2)}) async-start(), calls=%async_computation.7 | async-start | bytes 10027008 | tf_op jit(solution)/shard_map/all_gather | solution.py:119
  15.5 7.7 %copy-start.3 = (bf16[128,2048]{1,0:T(8,128)(2,1)S(1)}, bf16[128,2048]{1,0:T(8,128)(2,1)}, u32[]{:S(2)}) copy-start(bf16[128,2048]{1,0:T(8,128)(2,1)} %param.9) | copy-start | bytes 1572868
  15.5 28.4 %all-to-all-start = ((bf16[16,24,2048]{2,1,0:T(8,128)(2,1)}), bf16[16,24,2048]{2,1,0:T(8,128)(2,1)S(1)}, u32[]{:S(2)}, u32[]{:S(2)}) async-start(bf16[16,24,2048]{2,1,0:T(8,128)(2,1)} %bitcast.3), calls=%async_computation | async-start | bytes 3145728 | tf_op jit(solution)/shard_map/all_to_all | solution.py:124
  44.0 39.5 %all-to-all-start.2 = ((bf16[16,24,2048]{2,1,0:T(8,128)(2,1)}), bf16[16,24,2048]{2,1,0:T(8,128)(2,1)S(1)}, u32[]{:S(2)}, u32[]{:S(2)}) async-start(bf16[16,24,2048]{2,1,0:T(8,128)(2,1)} %bitcast.84), calls=%async_computation.2 | async-start | bytes 3145728 | tf_op jit(solution)/shard_map/all_to_all | solution.py:146
  49.3 117.7 %reduce-scatter.2.cloned.1.call-start = ((), (), s32[]{:S(2)}) async-start(), calls=%async_computation.8 | async-start | bytes 10027008 | tf_op jit(solution)/shard_map/reduce_scatter | solution.py:168
  87.7 1.9 copy-start.9
  87.7 1.9 copy-start.5
  87.7 1.9 copy-start.7
  97.9 1.1 copy-start.10
  103.5 6.8 %copy-start.4 = (bf16[128,2048]{1,0:T(8,128)(2,1)S(1)}, bf16[128,2048]{1,0:T(8,128)(2,1)}, u32[]{:S(2)}) copy-start(bf16[128,2048]{1,0:T(8,128)(2,1)} %param.9) | copy-start | bytes 1572868
  103.5 29.5 %all-to-all-start.1 = ((bf16[16,24,2048]{2,1,0:T(8,128)(2,1)}), bf16[16,24,2048]{2,1,0:T(8,128)(2,1)S(1)}, u32[]{:S(2)}, u32[]{:S(2)}) async-start(bf16[16,24,2048]{2,1,0:T(8,128)(2,1)} %bitcast.86), calls=%async_computation.1 | async-start | bytes 3145728 | tf_op jit(solution)/shard_map/all_to_all | solution.py:137
  110.2 1.6 copy-start.8
  137.8 6.2 %copy-start.2 = (bf16[128,2048]{1,0:T(8,128)(2,1)S(1)}, bf16[128,2048]{1,0:T(8,128)(2,1)}, u32[]{:S(2)}) copy-start(bf16[128,2048]{1,0:T(8,128)(2,1)} %param.8) | copy-start | bytes 1572868
  137.8 10.7 %copy-start.6 = (bf16[384,768]{1,0:T(8,128)(2,1)S(1)}, bf16[384,768]{1,0:T(8,128)(2,1)}, u32[]{:S(2)}) copy-start(bf16[384,768]{1,0:T(8,128)(2,1)} %copy-done.5) | copy-start | bytes 1769476
  144.9 10.4 %all-to-all-start.4 = ((f32[16,128,16]{1,2,0:T(8,128)}), f32[16,128,16]{1,2,0:T(8,128)S(1)}, u32[]{:S(2)}, u32[]{:S(2)}) async-start(f32[16,128,16]{1,2,0:T(8,128)} %bitcast.76), calls=%async_computation.4 | async-start | bytes 262144 | tf_op jit(solution)/shard_map/all_to_all | solution.py:23
  155.2 33.4 %all-to-all-start.3 = ((bf16[16,24,2048]{2,1,0:T(8,128)(2,1)}), bf16[16,24,2048]{2,1,0:T(8,128)(2,1)S(1)}, u32[]{:S(2)}, u32[]{:S(2)}) async-start(bf16[16,24,2048]{2,1,0:T(8,128)(2,1)} %bitcast.85), calls=%async_computation.3 | async-start | bytes 3145728 | tf_op jit(solution)/shard_map/all_to_all | solution.py:160
  160.7 24.7 %copy-start.12 = (s32[16]{0:T(128)S(1)}, s32[16]{0:T(128)}, u32[]{:S(2)}) copy-start(s32[16]{0:T(128)} %param.11) | copy-start | bytes 196
  169.0 33.6 %collective-permute-start.4 = (bf16[3,128,768]{2,1,0:T(8,128)(2,1)}, bf16[3,128,768]{2,1,0:T(8,128)(2,1)}, u32[]{:S(2)}, u32[]{:S(2)}) collective-permute-start(bf16[3,128,768]{2,1,0:T(8,128)(2,1)} %pad_maximum_fusion.1), channel_id=1, source_target_pairs={{0,1},{1,0},{2,3},{3,2},{4,5},{5,4},{6,7},{7,6},{8,9},{9,8},{10,11... | collective-permute-start | bytes 1769480 | tf_op jit(solution)/shard_map/ppermute | solution.py:9
  170.3 36.7 %collective-permute-start.5 = (bf16[3,128,768]{2,1,0:T(8,128)(2,1)}, bf16[3,128,768]{2,1,0:T(8,128)(2,1)}, u32[]{:S(2)}, u32[]{:S(2)}) collective-permute-start(bf16[3,128,768]{2,1,0:T(8,128)(2,1)} %pad_maximum_fusion.1), channel_id=1, source_target_pairs={{0,2},{1,3},{2,0},{3,1},{4,6},{5,7},{6,4},{7,5},{8,10},{9,11},{10,... | collective-permute-start | bytes 1769480 | tf_op jit(solution)/shard_map/ppermute | solution.py:9
  172.5 34.5 %collective-permute-start.6 = (bf16[3,128,768]{2,1,0:T(8,128)(2,1)}, bf16[3,128,768]{2,1,0:T(8,128)(2,1)}, u32[]{:S(2)}, u32[]{:S(2)}) collective-permute-start(bf16[3,128,768]{2,1,0:T(8,128)(2,1)} %pad_maximum_fusion.1), channel_id=1, source_target_pairs={{0,4},{1,5},{2,6},{3,7},{4,0},{5,1},{6,2},{7,3},{8,12},{9,13},{10,... | collective-permute-start | bytes 1769480 | tf_op jit(solution)/shard_map/ppermute | solution.py:9
  173.7 33.4 %collective-permute-start.7 = (bf16[3,128,768]{2,1,0:T(8,128)(2,1)}, bf16[3,128,768]{2,1,0:T(8,128)(2,1)}, u32[]{:S(2)}, u32[]{:S(2)}) collective-permute-start(bf16[3,128,768]{2,1,0:T(8,128)(2,1)} %pad_maximum_fusion.1), channel_id=1, source_target_pairs={{0,8},{1,9},{2,10},{3,11},{4,12},{5,13},{6,14},{7,15},{8,0},{9,1},... | collective-permute-start | bytes 1769480 | tf_op jit(solution)/shard_map/ppermute | solution.py:9
  176.2 5.1 %collective-permute-start = (f32[128,16]{0,1:T(8,128)S(1)}, f32[128,16]{0,1:T(8,128)S(1)}, u32[]{:S(2)}, u32[]{:S(2)}) collective-permute-start(f32[128,16]{0,1:T(8,128)S(1)} %reduce_sum.123), channel_id=1, source_target_pairs={{0,16},{16,0},{32,48},{48,32},{64,80},{80,64},{96,112},{112,96},{1... | collective-permute-start | bytes 24584 | tf_op jit(solution)/shard_map/ppermute | solution.py:9
  181.3 2.9 %collective-permute-start.1 = (f32[128,16]{0,1:T(8,128)S(1)}, f32[128,16]{0,1:T(8,128)S(1)}, u32[]{:S(2)}, u32[]{:S(2)}) collective-permute-start(f32[128,16]{0,1:T(8,128)S(1)} %add.85), channel_id=1, source_target_pairs={{0,32},{16,48},{32,0},{48,16},{64,96},{80,112},{96,64},{112,80},{1... | collective-permute-start | bytes 24584 | tf_op jit(solution)/shard_map/ppermute | solution.py:9
  184.2 11.9 %collective-permute-start.2 = (f32[128,16]{0,1:T(8,128)S(1)}, f32[128,16]{0,1:T(8,128)S(1)}, u32[]{:S(2)}, u32[]{:S(2)}) collective-permute-start(f32[128,16]{0,1:T(8,128)S(1)} %add.86), channel_id=1, source_target_pairs={{0,64},{16,80},{32,96},{48,112},{64,0},{80,16},{96,32},{112,48},{1... | collective-permute-start | bytes 24584 | tf_op jit(solution)/shard_map/ppermute | solution.py:9
  196.2 6.5 %collective-permute-start.3 = (f32[128,16]{0,1:T(8,128)S(1)}, f32[128,16]{0,1:T(8,128)S(1)}, u32[]{:S(2)}, u32[]{:S(2)}) collective-permute-start(f32[128,16]{0,1:T(8,128)S(1)} %add.87), channel_id=1, source_target_pairs={{0,128},{16,144},{32,160},{48,176},{64,192},{80,208},{96,224},{112... | collective-permute-start | bytes 24584 | tf_op jit(solution)/shard_map/ppermute | solution.py:9
  207.7 11.1 %all-to-all-start.5 = ((f32[16,128,16]{1,2,0:T(8,128)}), f32[16,128,16]{1,2,0:T(8,128)S(1)}, u32[]{:S(2)}, u32[]{:S(2)}) async-start(f32[16,128,16]{1,2,0:T(8,128)} %broadcast_in_dim.19), calls=%async_computation.6 | async-start | bytes 262144 | tf_op jit(solution)/shard_map/all_to_all | solution.py:15
Sparse Core Ops, SparseCore 0:
  9.9 64.9 all-gather.1
  98.1 68.8 reduce-scatter.1
where the time goes:
time: 227 us; the launch traced here: 226 us
  waiting for transfers between devices  73.9 us (33%)
  starting transfers between devices  48.5 us (21%)
  matrix products  34.8 us (15%)
  local copies, waits for them, and re-layouts  26.8 us (12%)
  other arithmetic  25.1 us (11%)
  between operations  17.1 us (8%)
    all_gather x1, waiting for transfers between devices, on_device(): gathered = lax.all_gather(held, 'dp', axis=1, tiled=True)  25.4 us
    all_to_all x1, waiting for transfers between devices, on_device(): lax.all_to_all(result, 'expert', split_axis=0, concat_axis=0, tiled=True)  16.2 us
    ppermute x8, starting transfers between devices, swapped(): lax.ppermute(array, axis, [(i, i ^ 1 << stride) for i in range(lax.axis_s...  15.1 us
    ppermute x8, waiting for transfers between devices, swapped(): lax.ppermute(array, axis, [(i, i ^ 1 << stride) for i in range(lax.axis_s...  11 us
    all_to_all x1, waiting for transfers between devices, on_device(): lax.all_to_all(outbox, 'expert', split_axis=0, concat_axis=0, tiled=True)  9.37 us
    all_to_all x1, starting transfers between devices, on_device(): lax.all_to_all(outbox, 'expert', split_axis=0, concat_axis=0, tiled=True)  7.7 us
    all_to_all x1, starting transfers between devices, on_device(): lax.all_to_all(result, 'expert', split_axis=0, concat_axis=0, tiled=True)  6.67 us
    reduce_scatter x1, waiting for transfers between devices, on_device(): lax.psum_scatter((jnp.concatenate(pieces, axis=1) * grad_scale).astype(jn...  6.22 us
  transfers between devices with their start and end apart: 16, of which 10 were waited for; matrix products, arithmetic and copies ran while one was open for 30% of the time, Pallas kernels for 0%

commit v1 on v0

--- a/solution.py
+++ b/solution.py
@@ -116,7 +116,9 @@
 
     gate_vals, gate_vjp = jax.vjp(gate_of, logits)
     held = jnp.concatenate([gate_weight, up_weight, down_weight], axis=0)
-    gathered = lax.all_gather(held, "dp", axis=1, tiled=True)
+    gathered = jnp.concatenate(
+        lax.all_to_all(jnp.stack([held] * lax.axis_size("dp")), "dp", 0, 0), axis=1
+    )
     gate_full, up_full, down_full = (gathered[0], gathered[1], gathered[2])
     slot_index = slot_numbers(expert_ids, labels, capacity, groups)
     spread = jnp.broadcast_to(tokens[:, None, :], (count, 2, width))

time: 227 us -> 441 us (1.94)
  the two profiles are of different devices: /device:TPU:1 before, /device:TPU:96 now
where the time goes in v1:
time: 441 us; the launch traced here: 433 us
  waiting for transfers between devices  272 us (62%)
  starting transfers between devices  50.4 us (11%)
  local copies, waits for them, and re-layouts  38.8 us (9%)
  matrix products  30.8 us (7%)
  other arithmetic  23.8 us (5%)
  between operations  17.3 us (4%)
    all_to_all x1, waiting for transfers between devices, on_device(): lax.all_to_all(jnp.stack([held] * lax.axis_size('dp')), 'dp', 0, 0)  195 us
    all_to_all x1, waiting for transfers between devices, on_device(): lax.all_to_all(outbox, 'expert', split_axis=0, concat_axis=0, tiled=True)  23.7 us
    all_to_all x1, waiting for transfers between devices, on_device(): lax.all_to_all(result, 'expert', split_axis=0, concat_axis=0, tiled=True)  15.5 us
    ppermute x8, starting transfers between devices, swapped(): lax.ppermute(array, axis, [(i, i ^ 1 << stride) for i in range(lax.axis_s...  15 us
    all_to_all x1, waiting for transfers between devices, on_device(): lax.all_to_all(d_outbox, 'expert', split_axis=0, concat_axis=0, tiled=True)  13.1 us
    ppermute x8, waiting for transfers between devices, swapped(): lax.ppermute(array, axis, [(i, i ^ 1 << stride) for i in range(lax.axis_s...  11.3 us
  transfers between devices with their start and end apart: 16, of which 11 were waited for; matrix products, arithmetic and copies ran while one was open for 15% of the time, Pallas kernels for 0%

profile of v1, /device:TPU:96, one launch (start us, length us, event | category | flops | bytes accessed | tf_op | source)
XLA Modules:
  0.0 433.5 jit_solution(15214440058266683133)
XLA Ops:
  9.4 1.7 broadcast_in_dim.14
  11.6 3.4 scatter_custom_fusion
  15.1 7.2 %all-to-all-start = ((bf16[16,24,2048]{2,1,0:T(8,128)(2,1)}), bf16[16,24,2048]{2,1,0:T(8,128)(2,1)S(1)}, u32[]{:S(2)}, u32[]{:S(2)}) async-start(bf16[16,24,2048]{2,1,0:T(8,128)(2,1)} %bitcast.3), calls=%async_computation | async-start | bytes 3145728 | tf_op jit(solution)/shard_map/all_to_all | solution.py:126
  22.4 23.7 %all-to-all-done = bf16[16,24,2048]{2,1,0:T(8,128)(2,1)S(1)} async-done(((bf16[16,24,2048]{2,1,0:T(8,128)(2,1)}), bf16[16,24,2048]{2,1,0:T(8,128)(2,1)S(1)}, u32[]{:S(2)}, u32[]{:S(2)}) %all-to-all-start) | async-done | bytes 1572896 | tf_op jit(solution)/shard_map/all_to_all | solution.py:126
  46.0 4.8 %stack.14 = bf16[16,3,128,768]{3,2,1,0:T(8,128)(2,1)} broadcast(bf16[3,128,768]{2,1,0:T(8,128)(2,1)S(1)} %pad_maximum_fusion), dimensions={1,2,3} | broadcast | bytes 10027008 | tf_op jit(solution)/shard_map/stack | solution.py:120
  50.8 7.8 %all-to-all-start.1 = ((bf16[16,3,128,768]{3,2,1,0:T(8,128)(2,1)}), bf16[16,3,128,768]{3,2,1,0:T(8,128)(2,1)}, u32[]{:S(2)}, u32[]{:S(2)}) async-start(bf16[16,3,128,768]{3,2,1,0:T(8,128)(2,1)} %stack.14), calls=%async_computation.1 | async-start | bytes 18874368 | tf_op jit(solution)/shard_map/all_to_all | solution.py:120
  58.6 2.4 mul.155
  61.0 3.7 mul.156
  65.3 4.6 %scatter_custom_fusion.1 = bf16[384,2048]{1,0:T(8,128)(2,1)} fusion(s32[256]{0:T(256)S(1)} %bitcast.91, f32[256,2048]{1,0:T(8,128)} %mul.156, f32[256]{0:T(256)S(1)} %div.42, bf16[]{:T(256)} %constant.16.clone.1), kind=kCustom, calls=%fused_computation.27 | custom fusion | flops 1048576 | bytes 3671042 | tf_op jit(solution)/shard_map/scatter | solution.py:59
  69.9 194.8 %all-to-all-done.1 = bf16[16,3,128,768]{3,2,1,0:T(8,128)(2,1)} async-done(((bf16[16,3,128,768]{3,2,1,0:T(8,128)(2,1)}), bf16[16,3,128,768]{3,2,1,0:T(8,128)(2,1)}, u32[]{:S(2)}, u32[]{:S(2)}) %all-to-all-start.1) | async-done | bytes 9437216 | tf_op jit(solution)/shard_map/all_to_all | solution.py:120
  264.7 3.9 all-to-all-start.3
  269.1 5.4 %fusion.22 = (bf16[1,16,128,768]{3,2,0,1:T(8,128)(2,1)}, bf16[1,16,128,768]{3,2,0,1:T(8,128)(2,1)S(1)}, bf16[1,16,128,768]{3,2,0,1:T(8,128)(2,1)S(1)}) fusion(bf16[3,16,128,768]{3,2,0,1:T(8,128)(2,1)} %bitcast.5), kind=kLoop, calls=%fused_computation.68 | loop fusion | bytes 18874368 | tf_op jit(solution)/shard_map/slice | solution.py:122
  274.5 2.9 fusion.24
  277.5 2.4 fusion.25
  279.9 13.1 %all-to-all-done.3 = bf16[16,24,2048]{2,1,0:T(8,128)(2,1)S(1)} async-done(((bf16[16,24,2048]{2,1,0:T(8,128)(2,1)}), bf16[16,24,2048]{2,1,0:T(8,128)(2,1)S(1)}, u32[]{:S(2)}, u32[]{:S(2)}) %all-to-all-start.3) | async-done | bytes 1572896 | tf_op jit(solution)/shard_map/all_to_all | solution.py:148
  293.0 4.2 multiply_convert_fusion.1
  297.3 1.9 fusion.27
  299.1 3.5 fusion.2
  302.6 4.9 %fusion = bf16[2048,2304]{1,0:T(8,128)(2,1)} fusion(f32[2048,768]{1,0:T(8,128)S(1)} %fusion.27, f32[2048,1536]{1,0:T(8,128)S(1)} %fusion.2), kind=kLoop, calls=%fused_computation.5 | loop fusion | flops 14155776 | bytes 28311552 | tf_op jit(solution)/shard_map/convert_element_type | solution.py:171
  307.6 1.9 copy-done.5
  309.5 3.6 convolution_convert_fusion
  313.1 4.0 all-to-all-start.2
  318.7 5.0 %fusion.26 = f32[384,2048]{1,0:T(8,128)} fusion(bf16[384,768]{1,0:T(8,128)(2,1)S(1)} %copy-done.11, bf16[2048,768]{1,0:T(8,128)(2,1)} %bitcast.84), kind=kOutput, calls=%fused_computation.72 | convolution fusion | flops 1207959552 | bytes 6881280 | tf_op jit(solution)/shard_map/dot_general | solution.py:78
  323.8 15.5 %all-to-all-done.2 = bf16[16,24,2048]{2,1,0:T(8,128)(2,1)S(1)} async-done(((bf16[16,24,2048]{2,1,0:T(8,128)(2,1)}), bf16[16,24,2048]{2,1,0:T(8,128)(2,1)S(1)}, u32[]{:S(2)}, u32[]{:S(2)}) %all-to-all-start.2) | async-done | bytes 1572896 | tf_op jit(solution)/shard_map/all_to_all | solution.py:139
  339.3 2.4 gather_fusion
  341.6 2.4 reshape.226
  344.1 6.0 %multiply_reduce_fusion = (f32[128,2]{1,0:T(8,128)S(1)}, bf16[128,2048]{1,0:T(8,128)(2,1)}) fusion(f32[128,2,2048]{2,1,0:T(2,128)S(1)} %reshape.226, f32[128,2048]{1,0:T(8,128)} %convert_element_type.54, f32[128,2]{1,0:T(8,128)S(1)} %copy.38), kind=kLoop, calls=%fused_computation.11 | loop fusion | flops 1834752 | bytes 3672064 | tf_op jit(solution)/shard_map/reduce_sum | solution.py:145
  351.1 3.5 all-to-all-start.5
  354.6 5.6 %add_convert_fusion = bf16[384,2048]{1,0:T(8,128)(2,1)} fusion(f32[384,2048]{1,0:T(8,128)} %fusion.26, bf16[384,768]{1,0:T(8,128)(2,1)S(1)} %copy-done.9, bf16[2048,768]{1,0:T(8,128)(2,1)} %bitcast.82), kind=kOutput, calls=%fused_computation.6 | convolution fusion | flops 1209532416 | bytes 8454144 | tf_op jit(solution)/shard_map/dot_general | solution.py:79
  360.3 2.1 all-to-all-done.5
  362.4 5.0 %all-to-all-start.4 = ((bf16[16,24,2048]{2,1,0:T(8,128)(2,1)}), bf16[16,24,2048]{2,1,0:T(8,128)(2,1)S(1)}, u32[]{:S(2)}, u32[]{:S(2)}) async-start(bf16[16,24,2048]{2,1,0:T(8,128)(2,1)} %bitcast.87), calls=%async_computation.4 | async-start | bytes 3145728 | tf_op jit(solution)/shard_map/all_to_all | solution.py:162
  367.5 6.0 %reduce-scatter.2.cloned.1.call-done = bf16[128,2304]{1,0:T(8,128)(2,1)} async-done(((bf16[2048,2304]{1,0:T(8,128)(2,1)}), bf16[128,2304]{1,0:T(8,128)(2,1)}) %reduce-scatter.2.cloned.1.call-update) | async-done | bytes 589840 | tf_op jit(solution)/shard_map/reduce_scatter | solution.py:170
  373.5 1.2 slice_bitcast_fusion.2
  375.6 1.4 collective-permute-start.4
  377.0 2.9 collective-permute-start.5
  379.8 1.5 collective-permute-start.6
  381.3 2.7 collective-permute-start.7
  384.0 2.3 collective-permute-start
  387.1 3.6 collective-permute-done.1
  394.8 2.3 gather_fusion.1
  397.1 2.4 reshape.227
  399.5 2.8 reduce_sum.118
  402.3 3.5 collective-permute-start.3
  406.9 3.0 collective-permute-done.3
  409.9 3.8 collective-permute-done.5
  414.4 3.5 all-to-all-start.6
  417.9 1.2 select_select_fusion
  420.0 5.7 %all-to-all-done.6 = f32[16,128,16]{1,2,0:T(8,128)S(1)} async-done(((f32[16,128,16]{1,2,0:T(8,128)}), f32[16,128,16]{1,2,0:T(8,128)S(1)}, u32[]{:S(2)}, u32[]{:S(2)}) %all-to-all-start.6) | async-done | bytes 131104 | tf_op jit(solution)/shard_map/all_to_all | solution.py:15
  (93 shorter events, 12.9 us)
Async XLA Ops:
  7.2 57.6 %copy-start = (bf16[2048,16]{0,1:T(8,128)(2,1)S(1)}, bf16[2048,16]{0,1:T(8,128)(2,1)}, u32[]{:S(2)}) copy-start(bf16[2048,16]{0,1:T(8,128)(2,1)} %param.12) | copy-start | bytes 196612
  15.1 7.2 %copy-start.13 = (bf16[1,128,768]{2,1,0:T(8,128)(2,1)S(1)}, bf16[1,128,768]{2,1,0:T(8,128)(2,1)}, u32[]{:S(2)}) copy-start(bf16[1,128,768]{2,1,0:T(8,128)(2,1)} %param.15) | copy-start | bytes 589828
  15.1 7.2 %copy-start.14 = (bf16[1,128,768]{2,1,0:T(8,128)(2,1)S(1)}, bf16[1,128,768]{2,1,0:T(8,128)(2,1)}, u32[]{:S(2)}) copy-start(bf16[1,128,768]{2,1,0:T(8,128)(2,1)} %param.14) | copy-start | bytes 589828
  15.1 7.2 %copy-start.15 = (bf16[1,128,768]{2,1,0:T(8,128)(2,1)S(1)}, bf16[1,128,768]{2,1,0:T(8,128)(2,1)}, u32[]{:S(2)}) copy-start(bf16[1,128,768]{2,1,0:T(8,128)(2,1)} %param.13) | copy-start | bytes 589828
  15.1 31.0 %all-to-all-start = ((bf16[16,24,2048]{2,1,0:T(8,128)(2,1)}), bf16[16,24,2048]{2,1,0:T(8,128)(2,1)S(1)}, u32[]{:S(2)}, u32[]{:S(2)}) async-start(bf16[16,24,2048]{2,1,0:T(8,128)(2,1)} %bitcast.3), calls=%async_computation | async-start | bytes 3145728 | tf_op jit(solution)/shard_map/all_to_all | solution.py:126
  50.8 7.8 %copy-start.6 = (bf16[128,2048]{1,0:T(8,128)(2,1)S(1)}, bf16[128,2048]{1,0:T(8,128)(2,1)}, u32[]{:S(2)}) copy-start(bf16[128,2048]{1,0:T(8,128)(2,1)} %param.9) | copy-start | bytes 1572868
  50.8 213.9 %all-to-all-start.1 = ((bf16[16,3,128,768]{3,2,1,0:T(8,128)(2,1)}), bf16[16,3,128,768]{3,2,1,0:T(8,128)(2,1)}, u32[]{:S(2)}, u32[]{:S(2)}) async-start(bf16[16,3,128,768]{3,2,1,0:T(8,128)(2,1)} %stack.14), calls=%async_computation.1 | async-start | bytes 18874368 | tf_op jit(solution)/shard_map/all_to_all | solution.py:120
  61.0 3.7 copy-start.1
  61.0 4.0 copy-start.16
  264.7 28.3 %all-to-all-start.3 = ((bf16[16,24,2048]{2,1,0:T(8,128)(2,1)}), bf16[16,24,2048]{2,1,0:T(8,128)(2,1)S(1)}, u32[]{:S(2)}, u32[]{:S(2)}) async-start(bf16[16,24,2048]{2,1,0:T(8,128)(2,1)} %bitcast.80), calls=%async_computation.3 | async-start | bytes 3145728 | tf_op jit(solution)/shard_map/all_to_all | solution.py:148
  268.6 104.9 %reduce-scatter.2.cloned.1.call-start = ((), (), s32[]{:S(2)}) async-start(), calls=%async_computation.8 | async-start | bytes 10027008 | tf_op jit(solution)/shard_map/reduce_scatter | solution.py:170
  274.5 2.9 copy-start.4
  274.5 3.0 copy-start.3
  297.2 1.9 copy-start.12
  297.2 1.9 copy-start.8
  297.2 1.9 copy-start.10
  307.6 1.9 copy-start.5
  313.1 4.2 copy-start.7
  313.1 26.2 %all-to-all-start.2 = ((bf16[16,24,2048]{2,1,0:T(8,128)(2,1)}), bf16[16,24,2048]{2,1,0:T(8,128)(2,1)S(1)}, u32[]{:S(2)}, u32[]{:S(2)}) async-start(bf16[16,24,2048]{2,1,0:T(8,128)(2,1)} %bitcast.88), calls=%async_computation.2 | async-start | bytes 3145728 | tf_op jit(solution)/shard_map/all_to_all | solution.py:139
  317.1 1.6 copy-start.11
  344.0 6.2 %copy-start.2 = (bf16[128,2048]{1,0:T(8,128)(2,1)S(1)}, bf16[128,2048]{1,0:T(8,128)(2,1)}, u32[]{:S(2)}) copy-start(bf16[128,2048]{1,0:T(8,128)(2,1)} %param.8) | copy-start | bytes 1572868
  344.0 10.6 %copy-start.9 = (bf16[384,768]{1,0:T(8,128)(2,1)S(1)}, bf16[384,768]{1,0:T(8,128)(2,1)}, u32[]{:S(2)}) copy-start(bf16[384,768]{1,0:T(8,128)(2,1)} %copy-done.8) | copy-start | bytes 1769476
  351.1 11.3 %all-to-all-start.5 = ((f32[16,128,16]{1,2,0:T(8,128)}), f32[16,128,16]{1,2,0:T(8,128)S(1)}, u32[]{:S(2)}, u32[]{:S(2)}) async-start(f32[16,128,16]{1,2,0:T(8,128)} %bitcast.72), calls=%async_computation.5 | async-start | bytes 262144 | tf_op jit(solution)/shard_map/all_to_all | solution.py:23
  362.4 32.4 %all-to-all-start.4 = ((bf16[16,24,2048]{2,1,0:T(8,128)(2,1)}), bf16[16,24,2048]{2,1,0:T(8,128)(2,1)S(1)}, u32[]{:S(2)}, u32[]{:S(2)}) async-start(bf16[16,24,2048]{2,1,0:T(8,128)(2,1)} %bitcast.87), calls=%async_computation.4 | async-start | bytes 3145728 | tf_op jit(solution)/shard_map/all_to_all | solution.py:162
  367.4 24.1 %copy-start.17 = (s32[16]{0:T(128)S(1)}, s32[16]{0:T(128)}, u32[]{:S(2)}) copy-start(s32[16]{0:T(128)} %param.11) | copy-start | bytes 196
  375.6 34.4 %collective-permute-start.4 = (bf16[3,128,768]{2,1,0:T(8,128)(2,1)}, bf16[3,128,768]{2,1,0:T(8,128)(2,1)}, u32[]{:S(2)}, u32[]{:S(2)}) collective-permute-start(bf16[3,128,768]{2,1,0:T(8,128)(2,1)} %pad_maximum_fusion.1), channel_id=1, source_target_pairs={{0,1},{1,0},{2,3},{3,2},{4,5},{5,4},{6,7},{7,6},{8,9},{9,8},{10,11... | collective-permute-start | bytes 1769480 | tf_op jit(solution)/shard_map/ppermute | solution.py:9
  377.0 36.8 %collective-permute-start.5 = (bf16[3,128,768]{2,1,0:T(8,128)(2,1)}, bf16[3,128,768]{2,1,0:T(8,128)(2,1)}, u32[]{:S(2)}, u32[]{:S(2)}) collective-permute-start(bf16[3,128,768]{2,1,0:T(8,128)(2,1)} %pad_maximum_fusion.1), channel_id=1, source_target_pairs={{0,2},{1,3},{2,0},{3,1},{4,6},{5,7},{6,4},{7,5},{8,10},{9,11},{10,... | collective-permute-start | bytes 1769480 | tf_op jit(solution)/shard_map/ppermute | solution.py:9
  379.8 33.9 %collective-permute-start.6 = (bf16[3,128,768]{2,1,0:T(8,128)(2,1)}, bf16[3,128,768]{2,1,0:T(8,128)(2,1)}, u32[]{:S(2)}, u32[]{:S(2)}) collective-permute-start(bf16[3,128,768]{2,1,0:T(8,128)(2,1)} %pad_maximum_fusion.1), channel_id=1, source_target_pairs={{0,4},{1,5},{2,6},{3,7},{4,0},{5,1},{6,2},{7,3},{8,12},{9,13},{10,... | collective-permute-start | bytes 1769480 | tf_op jit(solution)/shard_map/ppermute | solution.py:9
  381.3 32.4 %collective-permute-start.7 = (bf16[3,128,768]{2,1,0:T(8,128)(2,1)}, bf16[3,128,768]{2,1,0:T(8,128)(2,1)}, u32[]{:S(2)}, u32[]{:S(2)}) collective-permute-start(bf16[3,128,768]{2,1,0:T(8,128)(2,1)} %pad_maximum_fusion.1), channel_id=1, source_target_pairs={{0,8},{1,9},{2,10},{3,11},{4,12},{5,13},{6,14},{7,15},{8,0},{9,1},... | collective-permute-start | bytes 1769480 | tf_op jit(solution)/shard_map/ppermute | solution.py:9
  384.0 3.1 collective-permute-start
  387.1 3.7 collective-permute-start.1
  390.8 11.5 %collective-permute-start.2 = (f32[128,16]{0,1:T(8,128)S(1)}, f32[128,16]{0,1:T(8,128)S(1)}, u32[]{:S(2)}, u32[]{:S(2)}) collective-permute-start(f32[128,16]{0,1:T(8,128)S(1)} %add.86), channel_id=1, source_target_pairs={{0,64},{16,80},{32,96},{48,112},{64,0},{80,16},{96,32},{112,48},{1... | collective-permute-start | bytes 24584 | tf_op jit(solution)/shard_map/ppermute | solution.py:9
  402.3 7.7 %collective-permute-start.3 = (f32[128,16]{0,1:T(8,128)S(1)}, f32[128,16]{0,1:T(8,128)S(1)}, u32[]{:S(2)}, u32[]{:S(2)}) collective-permute-start(f32[128,16]{0,1:T(8,128)S(1)} %add.87), channel_id=1, source_target_pairs={{0,128},{16,144},{32,160},{48,176},{64,192},{80,208},{96,224},{112... | collective-permute-start | bytes 24584 | tf_op jit(solution)/shard_map/ppermute | solution.py:9
  414.4 11.3 %all-to-all-start.6 = ((f32[16,128,16]{1,2,0:T(8,128)}), f32[16,128,16]{1,2,0:T(8,128)S(1)}, u32[]{:S(2)}, u32[]{:S(2)}) async-start(f32[16,128,16]{1,2,0:T(8,128)} %broadcast_in_dim.19), calls=%async_computation.7 | async-start | bytes 262144 | tf_op jit(solution)/shard_map/all_to_all | solution.py:15
Sparse Core Ops, SparseCore 0:
  307.7 65.7 reduce-scatter.1
